TPU v7x, 32 devices: a whole 2x2x4 slice. The times are simulated.
32 devices in a mesh: group: 2 (over y), tm: 4 (over z), member: 2 (over x), sub: 2 (over core).
Axes of the slice: x: 2, y: 2, z: 4, core: 2. Of those that a mesh axis runs over, the one named last changes fastest.
Arguments:
- slices: float32 [8, 4, 2, 256, 256], P(('group', 'member', 'sub'), 'tm'), parts along dimension 0, may hold values from -1 to 1, as said below
- controls: float32 [4, 2, 256, 256], replicated, as said below
- target: float32 [4, 256, 256], P('group'), parts along dimension 0, may hold values from -1 to 1, as said below
Outputs:
- gradient: float32 [8, 4], P(('group', 'tm')), parts along dimension 0
There are 2 independent parts, one for each index of `group`. A program takes and returns all parts, laid end to end along the dimension named above; an argument that names none is the same for every part. Nothing has to cross between parts.
Inputs may be any that keep to these rules, and one draw needn't show every extreme that they name: Each slices[m, k] is a unitary matrix. `controls`: each control generator is Hermitian. The target is a unitary matrix.
All inputs are finite; a program needn't handle non-finite values.
Results may differ from a plain program's by a relative error of at most 0.0003.
Values sent between devices are 32-bit elements; how exact they have to be, the bound alone decides.
No kernel may reach another device: no remote copies, remote signals or barrier semaphores. Data moves between devices by JAX's collectives and lax.ppermute only.
A program may use at most 64 MiB of HBM per device.

v0:
```python
import jax
import jax.numpy as jnp
from jax import lax
from jax.sharding import PartitionSpec as P

HIGH = lax.Precision.HIGHEST


def cmul(left, right):
    real_part = jnp.matmul(left[..., 0, :, :], right[..., 0, :, :], precision=HIGH) - jnp.matmul(
        left[..., 1, :, :], right[..., 1, :, :], precision=HIGH
    )
    imag_part = jnp.matmul(left[..., 0, :, :], right[..., 1, :, :], precision=HIGH) + jnp.matmul(
        left[..., 1, :, :], right[..., 0, :, :], precision=HIGH
    )
    return jnp.stack([real_part, imag_part], axis=-3)


def cdagger(matrix):
    return jnp.stack(
        [jnp.swapaxes(matrix[..., 0, :, :], -1, -2), -jnp.swapaxes(matrix[..., 1, :, :], -1, -2)],
        axis=-3,
    )


def local_suffixes(identity_b):
    pieces = [identity_b]
    return jnp.stack(pieces, axis=1)


def tree_product(matrices):
    while matrices.shape[0] > 1:
        earlier_half = matrices[0::2]
        later_half = matrices[1::2]
        matrices = cmul(later_half, earlier_half)
    return matrices[0]


def per_device(slices, controls, target):
    members_here = slices.shape[0]
    order = slices.shape[-1]
    identity = jnp.stack(
        [jnp.eye(order, dtype=jnp.float32), jnp.zeros((order, order), jnp.float32)]
    )
    identity_b = jnp.broadcast_to(identity, (members_here, 2, order, order))
    target_dag = cdagger(target)
    current = slices[:, 0]
    prefixes = [current]
    local_prefix = jnp.stack(prefixes, axis=1)
    blocks = lax.axis_size("tm")
    position = lax.axis_index("tm")
    gathered = lax.all_gather(current, "tm", axis=0, tiled=True)
    gathered = gathered.reshape((blocks, members_here, 2, order, order))
    block_ids = jnp.arange(blocks, dtype=jnp.int32)[:, None, None, None, None]
    early_set = jnp.where(block_ids < position, gathered, identity_b[None])
    late_set = jnp.where(block_ids > position, gathered, identity_b[None])
    carry_in = tree_product(early_set)
    carry_out = tree_product(late_set)
    forward = cmul(local_prefix, carry_in[:, None])
    backward = cmul(carry_out[:, None], local_suffixes(identity_b))
    costate = cmul(cmul(forward, target_dag), backward)
    over_re = jnp.trace(costate[:, 0, 0], axis1=-2, axis2=-1)
    over_im = jnp.trace(costate[:, 0, 1], axis1=-2, axis2=-1)
    s_re = jnp.einsum(
        "mkab,jab->mkj", costate[:, :, 0], controls[:, 0], precision=HIGH
    ) + jnp.einsum("mkab,jab->mkj", costate[:, :, 1], controls[:, 1], precision=HIGH)
    s_im = jnp.einsum(
        "mkab,jab->mkj", costate[:, :, 1], controls[:, 0], precision=HIGH
    ) - jnp.einsum("mkab,jab->mkj", costate[:, :, 0], controls[:, 1], precision=HIGH)
    terms = over_re[:, None, None] * s_im - over_im[:, None, None] * s_re
    partial_value = jnp.sum(terms, axis=0)
    total = lax.psum(partial_value, ("member", "sub"))
    member_count = members_here * lax.axis_size("member") * lax.axis_size("sub")
    return total * (2.0 / member_count)


def solution(mesh):
    placed = (P(("group", "member", "sub"), "tm", None, None, None), P(), P("group", None, None))
    return jax.shard_map(
        per_device, mesh=mesh, in_specs=placed, out_specs=P(("group", "tm"), None), check_vma=False
    )
```

profile of v0, /device:TPU:0, one launch (start us, length us, event | category | flops | bytes accessed | tf_op | source)
XLA Modules:
  0.0 112.9 jit_solution(17755203991981334427)
XLA Ops:
  6.5 0.7 all-gather.3.cloned.1.call-update
  7.4 1.8 %slice_bitcast_fusion.1 = (f32[4,256,256]{2,1,0:T(8,128)S(1)}, f32[4,256,256]{2,1,0:T(8,128)S(1)}) fusion(f32[4,2,256,256]{3,2,1,0:T(8,128)} %param.4), kind=kLoop, calls=%fused_computation.31 | loop fusion | bytes 4194304 | tf_op jit(solution)/shard_map/squeeze | solution.py:68
  9.2 48.4 %all-gather.3.cloned.1.call-done = f32[4,1,2,256,256]{4,3,0,2,1:T(8,128)} async-done(((f32[1,1,2,256,256]{4,3,0,2,1:T(8,128)}), f32[4,1,2,256,256]{4,3,0,2,1:T(8,128)}) %all-gather.3.cloned.1.call-update) | async-done | bytes 2097168 | tf_op jit(solution)/shard_map/all_gather | solution.py:52
  57.6 2.1 %fusion.1 = (f32[4,1,2,256,256]{4,3,0,2,1:T(8,128)S(1)}, f32[4,1,2,256,256]{4,3,0,2,1:T(8,128)S(1)}) fusion(f32[4,1,2,256,256]{4,3,0,2,1:T(8,128)} %all-gather.3.cloned.1.call-done, f32[2,256,256]{2,1,0:T(8,128)S(1)} %get-tuple-element.14, pred[4]{0:T(512)(128)(4,1)S(1)} %get-tuple-element.19, pred[4]{0:T(512)(128)(4,1)S(1)} %get-tuple-element.20), kind=kLoop, calls=%fused_computation.3 | loop fusion | flops 1048576 | bytes 6815752 | tf_op jit(solution)/shard_map/jit(_where)/select_n | solution.py:56
  59.9 0.7 fusion.14
  60.6 0.7 fusion.15
  61.2 0.7 convolution_add_fusion
  61.9 0.7 convolution_subtract_fusion
  62.6 0.4 fusion.31
  63.3 0.4 convolution_subtract_fusion.4
  64.5 0.7 fusion.12
  65.2 0.7 fusion.13
  65.9 0.7 convolution_add_fusion.1
  66.5 0.7 convolution_subtract_fusion.1
  68.0 0.4 convolution_add_fusion.7
  68.4 0.4 convolution_subtract_fusion.7
  68.8 0.6 fusion.26
  69.4 0.6 fusion.24
  70.0 0.6 convolution_subtract_fusion.6
  70.6 0.6 fusion.16
  71.2 0.8 fusion.20
  73.0 0.6 convolution_add_fusion.6
  73.6 0.6 convolution_add_fusion.4
  74.2 0.6 convolution_subtract_fusion.5
  75.6 1.0 select_reduce_fusion
  76.5 1.0 select_reduce_fusion.1
  77.5 5.0 %convolution_bitcast_fusion = f32[4]{0:T(128)S(1)} fusion(f32[4,256,256]{2,1,0:T(8,128)S(1)} %get-tuple-element.8, f32[256,256,1]{1,0,2:T(8,128)S(1)} %bitcast.155), kind=kOutput, calls=%fused_computation.20 | convolution fusion | flops 3145728 | bytes 1310736 | tf_op jit(solution)/shard_map/mkab,jab->mkj/dot_general | solution.py:66
  82.5 5.0 %convolution_bitcast_fusion.2 = f32[4]{0:T(128)S(1)} fusion(f32[4,256,256]{2,1,0:T(8,128)S(1)} %get-tuple-element.8, f32[256,256,1]{1,0,2:T(8,128)S(1)} %bitcast.157), kind=kOutput, calls=%fused_computation.22 | convolution fusion | flops 3145728 | bytes 1310736 | tf_op jit(solution)/shard_map/mkab,jab->mkj/dot_general | solution.py:69
  87.5 5.6 %fusion.7 = f32[4]{0:T(128)S(1)} fusion(f32[4]{0:T(128)S(1)} %convolution_bitcast_fusion, f32[4,256,256]{2,1,0:T(8,128)S(1)} %get-tuple-element.7, f32[256,256,1]{1,0,2:T(8,128)S(1)} %bitcast.158, f32[]{:T(128)} %get-tuple-element.15), kind=kOutput, calls=%fused_computation.29 | convolution fusion | flops 3145736 | bytes 1310756 | tf_op jit(solution)/shard_map/mkab,jab->mkj/dot_general | solution.py:64
  93.1 5.6 %fusion.5 = f32[1,4]{1,0:T(1,128)S(1)} fusion(f32[4]{0:T(128)S(1)} %fusion.7, f32[4]{0:T(128)S(1)} %convolution_bitcast_fusion.2, f32[4,256,256]{2,1,0:T(8,128)S(1)} %get-tuple-element.7, f32[256,256,1]{1,0,2:T(8,128)S(1)} %bitcast.156, f32[]{:T(128)} %get-tuple-element.17), kind=kOutput, calls=%fused_computation.27 | convolution fusion | flops 3145740 | bytes 1310772 | tf_op jit(solution)/shard_map/mkab,jab->mkj/dot_general | solution.py:67
  98.7 6.8 %psum.7 = f32[1,4]{1,0:T(1,128)S(1)} all-reduce(f32[1,4]{1,0:T(1,128)S(1)} %fusion.5), channel_id=1, replica_groups=mesh['group'=2,'tm'=4,'member'=2,'sub'=2] {'member','sub'}, use_global_device_ids=true, to_apply=%region_2.3 | all-reduce | flops 4 | bytes 32 | tf_op jit(solution)/shard_map/psum | solution.py:72
  105.5 0.5 broadcast_multiply_fusion
  (20 shorter events, 4.0 us)
Async XLA Ops:
  6.5 51.1 %all-gather.3.cloned.1.call-start = ((), (), s32[]{:S(2)}) async-start(), calls=%async_computation | async-start | bytes 2621440 | tf_op jit(solution)/shard_map/all_gather | solution.py:52
  67.2 1.6 %copy-start = (f32[1,1,2,256,256]{4,3,2,1,0:T(8,128)S(1)}, f32[1,1,2,256,256]{4,3,2,1,0:T(8,128)}, u32[]{:S(2)}) copy-start(f32[1,1,2,256,256]{4,3,2,1,0:T(8,128)} %param.3) | copy-start | bytes 1572868
  68.4 2.2 %copy-start.1 = (f32[2,256,256]{2,1,0:T(8,128)S(1)}, f32[2,256,256]{2,1,0:T(8,128)}, u32[]{:S(2)}) copy-start(f32[2,256,256]{2,1,0:T(8,128)} %param.5) | copy-start | bytes 1572868
Sparse Core Ops, SparseCore 0:
  8.9 48.6 all-gather.2
where the time goes:
time: 113 us
  waiting for transfers between devices  49.1 us (43%)
  matrix products  38.3 us (34%)
  between operations  13.7 us (12%)
  blocking collectives  6.82 us (6%)
  other arithmetic  2.67 us (2%)
  local copies, waits for them, and re-layouts  2.22 us (2%)
    all_gather x1, waiting for transfers between devices, per_device(): gathered = lax.all_gather(current, 'tm', axis=0, tiled=True)  48.4 us
    psum x1, blocking collectives, per_device(): total = lax.psum(partial_value, ('member', 'sub'))  6.82 us
    dot_general x1, matrix products, per_device(): jnp.einsum('mkab,jab->mkj', costate[:, :, 1], controls[:, 0], precision=H...  5.59 us
    dot_general x1, matrix products, per_device(): jnp.einsum('mkab,jab->mkj', costate[:, :, 0], controls[:, 0], precision=H...  5.59 us
    dot_general x1, matrix products, per_device(): jnp.einsum('mkab,jab->mkj', costate[:, :, 0], controls[:, 1], precision=H...  4.99 us
    dot_general x1, matrix products, per_device(): jnp.einsum('mkab,jab->mkj', costate[:, :, 1], controls[:, 1], precision=H...  4.97 us
    dot_general x8, matrix products, cmul(): jnp.matmul(left[..., 1, :, :], right[..., 1, :, :], precision=HIGH)  4.55 us
    dot_general x8, matrix products, cmul(): jnp.matmul(left[..., 1, :, :], right[..., 0, :, :], precision=HIGH)  4.55 us
  transfers between devices with their start and end apart: 1, of which 1 were waited for; matrix products, arithmetic and copies ran while one was open for 2% of the time, Pallas kernels for 0%

commit v1 on v0

--- a/solution.py
+++ b/solution.py
@@ -37,6 +37,29 @@
 
 
 def per_device(slices, controls, target):
+
+    def register_tracks_now(local, peer_axis):
+        met_up = lax.axis_index(peer_axis)
+        before = lax.axis_size(peer_axis)
+        q_next, v_now, b_now = (before, met_up, local.shape[0])
+        store = tuple(((i0, (i0 + 1) % q_next) for i0 in range(q_next)))
+        pages = tuple(((i0, (i0 - 1) % q_next) for i0 in range(q_next)))
+        plain = jnp.zeros((*local.shape[:0], q_next * b_now, *local.shape[1:]), local.dtype)
+        x_new = step_out = local
+        next_value = q_next // 2
+        plain = lax.dynamic_update_slice_in_dim(plain, local, v_now * b_now, axis=0)
+        for m in range(1, next_value + 1):
+            x_new = lax.ppermute(x_new, axis_name=peer_axis, perm=store)
+            plain = lax.dynamic_update_slice_in_dim(
+                plain, x_new, (v_now - m) % q_next * b_now, axis=0
+            )
+            if m < q_next - next_value:
+                step_out = lax.ppermute(step_out, peer_axis, perm=pages)
+                plain = lax.dynamic_update_slice_in_dim(
+                    plain, step_out, (v_now + m) % q_next * b_now, axis=0
+                )
+        return plain
+
     members_here = slices.shape[0]
     order = slices.shape[-1]
     identity = jnp.stack(
@@ -49,7 +72,7 @@
     local_prefix = jnp.stack(prefixes, axis=1)
     blocks = lax.axis_size("tm")
     position = lax.axis_index("tm")
-    gathered = lax.all_gather(current, "tm", axis=0, tiled=True)
+    gathered = register_tracks_now(current, "tm")
     gathered = gathered.reshape((blocks, members_here, 2, order, order))
     block_ids = jnp.arange(blocks, dtype=jnp.int32)[:, None, None, None, None]
     early_set = jnp.where(block_ids < position, gathered, identity_b[None])

time: 113 us -> 90.8 us (0.80)
  waiting for transfers between devices: 49.1 us -> 31.5 us
  between operations: 13.7 us -> 0.36 us
  starting transfers between devices: 0.01 us -> 6.67 us
  local copies, waits for them, and re-layouts: 2.22 us -> 6.8 us
  other arithmetic: 2.67 us -> 1.08 us
  blocking collectives: 6.82 us -> 5.65 us
    all_gather x1 -> x0, waiting for transfers between devices: 48.4 us -> none  [per_device(): gathered = lax.all_gather(current, 'tm', axis=0, tiled=True)]
    ppermute x0 -> x3, waiting for transfers between devices: none -> 31.5 us  [the longest x2 31.5 us: register_tracks_now(): x_new = lax.ppermute(x_new, axis_name=peer_axis, perm=store)]
    ppermute x0 -> x3, starting transfers between devices: none -> 6.67 us  [the longest x1 5.05 us: register_tracks_now(): step_out = lax.ppermute(step_out, peer_axis, perm=pages)]
    dynamic_update_slice x0 -> x4, local copies, waits for them, and re-layouts: none -> 3.32 us  [the longest x2 2.19 us: register_tracks_now(): lax.dynamic_update_slice_in_dim(plain, x_new, (v_now - m) % q_next * b_no...]
    select_n x1, other arithmetic: 2.05 us -> 0.47 us  [per_device(): late_set = jnp.where(block_ids > position, gathered, identity_b[None])]
    unnamed x4 -> x10, local copies, waits for them, and re-layouts: 0.01 us -> 1.37 us
    psum x1, blocking collectives: 6.82 us -> 5.65 us  [per_device(): total = lax.psum(partial_value, ('member', 'sub'))]
  transfers between devices with their start and end apart: 1 -> 3, of which waited for: 1 -> 2; matrix products, arithmetic and copies ran while one was open for 2% -> 4% of each run, Pallas kernels for 0% -> 0%
where the time goes in v1:
time: 90.8 us; the launch traced here: 90.5 us
  matrix products  38.4 us (42%)
  waiting for transfers between devices  31.5 us (35%)
  local copies, waits for them, and re-layouts  6.8 us (7%)
  starting transfers between devices  6.67 us (7%)
  blocking collectives  5.65 us (6%)
  other arithmetic  1.08 us (1%)
    ppermute x2, waiting for transfers between devices, register_tracks_now(): x_new = lax.ppermute(x_new, axis_name=peer_axis, perm=store)  31.5 us
    dot_general x1, matrix products, per_device(): jnp.einsum('mkab,jab->mkj', costate[:, :, 1], controls[:, 0], precision=H...  5.65 us
    psum x1, blocking collectives, per_device(): total = lax.psum(partial_value, ('member', 'sub'))  5.65 us
    dot_general x1, matrix products, per_device(): jnp.einsum('mkab,jab->mkj', costate[:, :, 0], controls[:, 0], precision=H...  5.59 us
    ppermute x1, starting transfers between devices, register_tracks_now(): step_out = lax.ppermute(step_out, peer_axis, perm=pages)  5.05 us
    dot_general x1, matrix products, per_device(): jnp.einsum('mkab,jab->mkj', costate[:, :, 0], controls[:, 1], precision=H...  4.99 us
    dot_general x1, matrix products, per_device(): jnp.einsum('mkab,jab->mkj', costate[:, :, 1], controls[:, 1], precision=H...  4.97 us
    dot_general x8, matrix products, cmul(): jnp.matmul(left[..., 1, :, :], right[..., 1, :, :], precision=HIGH)  4.61 us
  transfers between devices with their start and end apart: 3, of which 2 were waited for; matrix products, arithmetic and copies ran while one was open for 4% of the time, Pallas kernels for 0%

profile of v1, /device:TPU:0, one launch (start us, length us, event | category | flops | bytes accessed | tf_op | source)
XLA Modules:
  0.0 90.5 jit_solution(85274664777565794)
XLA Ops:
  0.0 5.0 %collective-permute-start.1 = (f32[1,2,256,256]{3,2,1,0:T(8,128)}, f32[1,2,256,256]{3,2,1,0:T(8,128)}, u32[]{:S(2)}, u32[]{:S(2)}) collective-permute-start(f32[1,2,256,256]{3,2,1,0:T(8,128)} %bitcast.155), channel_id=1, source_target_pairs={{0,12},{4,0},{8,4},{12,8},{1,13},{5,1},{9,5},{13,9},{2,14},{6,2},{... | collective-permute-start | bytes 1572872 | tf_op jit(solution)/shard_map/ppermute | solution.py:57
  5.3 1.3 %copy-done.1 = f32[4,2,256,256]{3,2,1,0:T(8,128)S(1)} copy-done((f32[4,2,256,256]{3,2,1,0:T(8,128)S(1)}, f32[4,2,256,256]{3,2,1,0:T(8,128)}, u32[]{:S(2)}) %copy-start.1) | copy-done | bytes 2097176
  6.6 1.5 %slice_bitcast_fusion.1 = (f32[4,256,256]{2,1,0:T(8,128)}, f32[4,256,256]{2,1,0:T(8,128)}) fusion(f32[4,2,256,256]{3,2,1,0:T(8,128)S(1)} %copy-done.1), kind=kLoop, calls=%fused_computation.27 | loop fusion | bytes 4194304 | tf_op jit(solution)/shard_map/squeeze | solution.py:91
  8.3 20.4 %collective-permute-done = f32[1,2,256,256]{3,2,1,0:T(8,128)} collective-permute-done((f32[1,2,256,256]{3,2,1,0:T(8,128)}, f32[1,2,256,256]{3,2,1,0:T(8,128)}, u32[]{:S(2)}, u32[]{:S(2)}) %collective-permute-start) | collective-permute-done | bytes 524320 | tf_op jit(solution)/shard_map/ppermute | solution.py:52
  28.7 1.6 %collective-permute-start.2 = (f32[1,2,256,256]{3,2,1,0:T(8,128)}, f32[1,2,256,256]{3,2,1,0:T(8,128)}, u32[]{:S(2)}, u32[]{:S(2)}) collective-permute-start(f32[1,2,256,256]{3,2,1,0:T(8,128)} %collective-permute-done), channel_id=1, source_target_pairs={{0,4},{4,8},{8,12},{12,0},{1,5},{5,9},{9,13},{13,1},{2,6},{6,10},{... | collective-permute-start | bytes 1572872 | tf_op jit(solution)/shard_map/ppermute | solution.py:52
  30.3 1.1 %bitcast_dynamic-update-slice_fusion.1 = f32[4,1,2,256,256]{4,3,0,2,1:T(8,128)S(1)} fusion(f32[4,1,2,256,256]{4,3,0,2,1:T(8,128)S(1)} %bitcast_dynamic-update-slice_fusion.3, s32[]{:T(128)S(6)} %select_n.50, f32[1,2,256,256]{3,2,1,0:T(8,128)} %collective-permute-done), kind=kLoop, calls=%fused_computation.45 | loop fusion | bytes 1048580 | tf_op jit(solution)/shard_map/dynamic_update_slice | solution.py:53
  31.4 1.1 %bitcast_dynamic-update-slice_fusion = f32[4,1,2,256,256]{4,3,0,2,1:T(8,128)S(1)} fusion(f32[4,1,2,256,256]{4,3,0,2,1:T(8,128)S(1)} %bitcast_dynamic-update-slice_fusion.1, s32[]{:T(128)S(6)} %select_n.52, f32[1,2,256,256]{3,2,1,0:T(8,128)} %collective-permute-done.1), kind=kLoop, calls=%fused_computation.44 | loop fusion | bytes 1048580 | tf_op jit(solution)/shard_map/dynamic_update_slice | solution.py:58
  32.5 11.1 %collective-permute-done.2 = f32[1,2,256,256]{3,2,1,0:T(8,128)} collective-permute-done((f32[1,2,256,256]{3,2,1,0:T(8,128)}, f32[1,2,256,256]{3,2,1,0:T(8,128)}, u32[]{:S(2)}, u32[]{:S(2)}) %collective-permute-start.2) | collective-permute-done | bytes 524320 | tf_op jit(solution)/shard_map/ppermute | solution.py:52
  43.6 1.1 %bitcast_dynamic-update-slice_fusion.2 = f32[4,1,2,256,256]{4,3,0,2,1:T(8,128)S(1)} fusion(f32[4,1,2,256,256]{4,3,0,2,1:T(8,128)S(1)} %bitcast_dynamic-update-slice_fusion, s32[]{:T(128)S(6)} %select_n.54, f32[1,2,256,256]{3,2,1,0:T(8,128)} %collective-permute-done.2), kind=kLoop, calls=%fused_computation.46 | loop fusion | bytes 1048580 | tf_op jit(solution)/shard_map/dynamic_update_slice | solution.py:53
  45.4 0.7 fusion.12
  46.1 0.7 fusion.13
  46.7 0.7 convolution_add_fusion
  47.4 0.7 convolution_subtract_fusion
  50.0 0.7 fusion.10
  50.7 0.7 fusion.11
  51.4 0.7 convolution_add_fusion.1
  52.0 0.7 convolution_subtract_fusion.1
  54.3 0.6 fusion.24
  54.9 0.6 fusion.22
  55.5 0.6 convolution_subtract_fusion.6
  56.1 0.6 fusion.14
  56.7 0.8 fusion.18
  58.5 0.6 convolution_add_fusion.6
  59.1 0.6 convolution_add_fusion.4
  59.7 0.6 convolution_subtract_fusion.5
  61.1 1.0 %select_reduce_fusion = (f32[]{:T(128)}, f32[256,256]{1,0:T(8,128)S(1)}) fusion(f32[256,256]{1,0:T(8,128)S(1)} %fusion.45, f32[256,256]{1,0:T(8,128)S(1)} %convolution_add_fusion.4, f32[256,256]{1,0:T(8,128)S(1)} %convolution_subtract_fusion.3), kind=kOutput, calls=%fused_computation.72 | convolution fusion | flops 201588736 | bytes 1048580 | tf_op jit(solution)/shard_map/dot_general | solution.py:13
  62.0 1.0 %select_reduce_fusion.1 = (f32[]{:T(128)}, f32[256,256]{1,0:T(8,128)S(1)}) fusion(f32[256,256]{1,0:T(8,128)S(1)} %fusion.44, f32[256,256]{1,0:T(8,128)S(1)} %convolution_add_fusion.4, f32[256,256]{1,0:T(8,128)S(1)} %convolution_add_fusion.3), kind=kOutput, calls=%fused_computation.73 | convolution fusion | flops 201588736 | bytes 1048580 | tf_op jit(solution)/shard_map/dot_general | solution.py:10
  63.1 5.0 %convolution_bitcast_fusion = f32[4]{0:T(128)S(1)} fusion(f32[4,256,256]{2,1,0:T(8,128)S(1)} %copy-done.4, f32[256,256,1]{1,0,2:T(8,128)S(1)} %bitcast.157), kind=kOutput, calls=%fused_computation.16 | convolution fusion | flops 3145728 | bytes 1310736 | tf_op jit(solution)/shard_map/mkab,jab->mkj/dot_general | solution.py:89
  68.1 5.0 %convolution_bitcast_fusion.2 = f32[4]{0:T(128)S(1)} fusion(f32[4,256,256]{2,1,0:T(8,128)S(1)} %copy-done.4, f32[256,256,1]{1,0,2:T(8,128)S(1)} %bitcast.159), kind=kOutput, calls=%fused_computation.18 | convolution fusion | flops 3145728 | bytes 1310736 | tf_op jit(solution)/shard_map/mkab,jab->mkj/dot_general | solution.py:92
  73.1 5.6 %fusion.5 = f32[4]{0:T(128)S(1)} fusion(f32[4]{0:T(128)S(1)} %convolution_bitcast_fusion, f32[4,256,256]{2,1,0:T(8,128)S(1)} %copy-done.3, f32[256,256,1]{1,0,2:T(8,128)S(1)} %bitcast.160, f32[]{:T(128)} %get-tuple-element.15), kind=kOutput, calls=%fused_computation.25 | convolution fusion | flops 3145736 | bytes 1310756 | tf_op jit(solution)/shard_map/mkab,jab->mkj/dot_general | solution.py:87
  78.6 5.7 %fusion.3 = f32[1,4]{1,0:T(1,128)S(1)} fusion(f32[4]{0:T(128)S(1)} %fusion.5, f32[4]{0:T(128)S(1)} %convolution_bitcast_fusion.2, f32[4,256,256]{2,1,0:T(8,128)S(1)} %copy-done.3, f32[256,256,1]{1,0,2:T(8,128)S(1)} %bitcast.158, f32[]{:T(128)} %get-tuple-element.17), kind=kOutput, calls=%fused_computation.23 | convolution fusion | flops 3145740 | bytes 1310772 | tf_op jit(solution)/shard_map/mkab,jab->mkj/dot_general | solution.py:90
  84.3 5.6 %psum.7 = f32[1,4]{1,0:T(1,128)S(1)} all-reduce(f32[1,4]{1,0:T(1,128)S(1)} %fusion.3), channel_id=1, replica_groups=mesh['group'=2,'tm'=4,'member'=2,'sub'=2] {'member','sub'}, use_global_device_ids=true, to_apply=%region_2.3 | all-reduce | flops 4 | bytes 32 | tf_op jit(solution)/shard_map/psum | solution.py:95
  (34 shorter events, 6.7 us)
Async XLA Ops:
  0.0 5.2 %copy-start = (f32[1,1,2,256,256]{4,3,2,1,0:T(8,128)S(1)}, f32[1,1,2,256,256]{4,3,2,1,0:T(8,128)}, u32[]{:S(2)}) copy-start(f32[1,1,2,256,256]{4,3,2,1,0:T(8,128)} %param.3) | copy-start | bytes 1572868
  0.0 31.4 %collective-permute-start.1 = (f32[1,2,256,256]{3,2,1,0:T(8,128)}, f32[1,2,256,256]{3,2,1,0:T(8,128)}, u32[]{:S(2)}, u32[]{:S(2)}) collective-permute-start(f32[1,2,256,256]{3,2,1,0:T(8,128)} %bitcast.155), channel_id=1, source_target_pairs={{0,12},{4,0},{8,4},{12,8},{1,13},{5,1},{9,5},{13,9},{2,14},{6,2},{... | collective-permute-start | bytes 1572872 | tf_op jit(solution)/shard_map/ppermute | solution.py:57
  5.1 23.6 %collective-permute-start = (f32[1,2,256,256]{3,2,1,0:T(8,128)}, f32[1,2,256,256]{3,2,1,0:T(8,128)}, u32[]{:S(2)}, u32[]{:S(2)}) collective-permute-start(f32[1,2,256,256]{3,2,1,0:T(8,128)} %bitcast.156), channel_id=1, source_target_pairs={{0,4},{4,8},{8,12},{12,0},{1,5},{5,9},{9,13},{13,1},{2,6},{6,10},{... | collective-permute-start | bytes 1572872 | tf_op jit(solution)/shard_map/ppermute | solution.py:52
  5.1 1.6 %copy-start.1 = (f32[4,2,256,256]{3,2,1,0:T(8,128)S(1)}, f32[4,2,256,256]{3,2,1,0:T(8,128)}, u32[]{:S(2)}) copy-start(f32[4,2,256,256]{3,2,1,0:T(8,128)} %param.4) | copy-start | bytes 6291460
  28.7 14.9 %collective-permute-start.2 = (f32[1,2,256,256]{3,2,1,0:T(8,128)}, f32[1,2,256,256]{3,2,1,0:T(8,128)}, u32[]{:S(2)}, u32[]{:S(2)}) collective-permute-start(f32[1,2,256,256]{3,2,1,0:T(8,128)} %collective-permute-done), channel_id=1, source_target_pairs={{0,4},{4,8},{8,12},{12,0},{1,5},{5,9},{9,13},{13,1},{2,6},{6,10},{... | collective-permute-start | bytes 1572872 | tf_op jit(solution)/shard_map/ppermute | solution.py:52
  53.9 2.2 %copy-start.2 = (f32[2,256,256]{2,1,0:T(8,128)S(1)}, f32[2,256,256]{2,1,0:T(8,128)}, u32[]{:S(2)}) copy-start(f32[2,256,256]{2,1,0:T(8,128)} %param.5) | copy-start | bytes 1572868
  60.3 2.8 %copy-start.4 = (f32[4,256,256]{2,1,0:T(8,128)S(1)}, f32[4,256,256]{2,1,0:T(8,128)}, u32[]{:S(2)}) copy-start(f32[4,256,256]{2,1,0:T(8,128)} %get-tuple-element.8) | copy-start | bytes 3145732
  63.1 10.0 %copy-start.3 = (f32[4,256,256]{2,1,0:T(8,128)S(1)}, f32[4,256,256]{2,1,0:T(8,128)}, u32[]{:S(2)}) copy-start(f32[4,256,256]{2,1,0:T(8,128)} %get-tuple-element.7) | copy-start | bytes 3145732
